TPU v7x, 32 devices: a whole 2x2x4 slice. The times are simulated.
32 devices in a mesh: gx: 8 (over z, x), gy: 4 (over y, core).
Axes of the slice: x: 2, y: 2, z: 4, core: 2. Of those that a mesh axis runs over, the one named last changes fastest.
Arguments:
- inputs: bfloat16 [3, 256, 8192], P(None, 'gy', 'gx'), may hold values from -600 to 600
- norm_gain: bfloat16 [8192], P('gx'), may hold values from 0.099609375 to 1.8984375
- query_weight: bfloat16 [8192, 8192], P('gx', 'gy'), may hold values from -0.0625 to 0.0625
- key_weight: bfloat16 [8192, 1024], P('gx', 'gy'), may hold values from -0.0625 to 0.0625
- value_weight: bfloat16 [8192, 1024], P('gx', 'gy'), may hold values from -0.0625 to 0.0625
- output_weight: bfloat16 [8192, 8192], P('gy', 'gx'), may hold values from -0.0625 to 0.0625
- query_down: bfloat16 [256, 8192, 64], P('gy', 'gx'), may hold values from -0.0625 to 0.0625
- query_up: bfloat16 [256, 64, 8192], P('gx', None, 'gy'), may hold values from -0.75 to 0.75
- output_down: bfloat16 [256, 8192, 64], P('gx', 'gy'), may hold values from -0.0625 to 0.0625
- output_up: bfloat16 [256, 64, 8192], P('gy', None, 'gx'), may hold values from -0.75 to 0.75
- block_adapter: int32 [2], replicated, may hold values from 0 to 255
- cache_lengths: int32 [256], P(('gx', 'gy')), may hold values from 1 to 256, as said below
- cache_keys: bfloat16 [256, 256, 1024], P(('gx', 'gy')), may hold values from -160 to 160
- cache_values: bfloat16 [256, 256, 1024], P(('gx', 'gy')), may hold values from -6 to 6
Outputs:
- block_output: bfloat16 [3, 256, 8192], P(None, 'gy', 'gx')
Inputs may be any that keep to these rules, and one draw needn't show every extreme that they name: `cache_lengths`: some request has exactly 256 cached positions.
All inputs are finite; a program needn't handle non-finite values.
Results may differ from a plain program's by a relative error of at most 0.012.
The roundings to bfloat16 on the way count: a program that leaves them out, or rounds other values in their place, can miss the bound.
Values may be sent and summed in bfloat16 or wider, within the bound.
No kernel may reach another device: no remote copies, remote signals or barrier semaphores. Data moves between devices by JAX's collectives and lax.ppermute only.
A program may use at most 192 MiB of HBM per device.

v0:
```python
import jax
import jax.numpy as jnp
from jax import lax
from jax.sharding import PartitionSpec as P

D = 8192
QUERY_HEADS = 64
KEY_VALUE_HEADS = 8
HEAD_FEATURES = 128
BLOCK = 128
STEPS = 3
EPS = 1e-05
THETA = 500000.0


def rotary_embedding(values_in, token_positions):
    half_size = values_in.shape[-1] // 2
    exponent = jnp.arange(half_size, dtype=jnp.float32) * 2.0 / values_in.shape[-1]
    frequency = THETA ** (-exponent)
    angles = token_positions.astype(jnp.float32)[:, None] * frequency[None, :]
    cosine = jnp.cos(angles)[:, None, :]
    sine_part = jnp.sin(angles)[:, None, :]
    lower = values_in[..., :half_size]
    upper = values_in[..., half_size:]
    return jnp.concatenate(
        [lower * cosine - upper * sine_part, upper * cosine + lower * sine_part], axis=-1
    )


def pick_adapters(table, adapter_ids, first_id):
    table_count = table.shape[0]
    wanted = first_id + jnp.arange(table_count, dtype=jnp.int32)
    onehot = (adapter_ids[:, None] == wanted[None, :]).astype(table.dtype)
    flat_table = table.reshape(table_count, -1)
    picked = jnp.dot(onehot, flat_table, preferred_element_type=jnp.float32).astype(table.dtype)
    return picked.reshape((adapter_ids.shape[0],) + table.shape[1:])


def attend(
    query_rows, previous_keys, previous_values, incoming_keys, incoming_values, lengths, step_index
):
    count_of_rows = query_rows.shape[0]
    context_window = previous_keys.shape[1]
    grouped_heads = query_rows.reshape(
        count_of_rows, KEY_VALUE_HEADS, QUERY_HEADS // KEY_VALUE_HEADS, HEAD_FEATURES
    )
    keys_previous = previous_keys.reshape(
        count_of_rows, context_window, KEY_VALUE_HEADS, HEAD_FEATURES
    )
    values_previous = previous_values.reshape(
        count_of_rows, context_window, KEY_VALUE_HEADS, HEAD_FEATURES
    )
    keys_incoming = incoming_keys.reshape(count_of_rows, -1, KEY_VALUE_HEADS, HEAD_FEATURES)
    values_incoming = incoming_values.reshape(count_of_rows, -1, KEY_VALUE_HEADS, HEAD_FEATURES)
    factor = HEAD_FEATURES ** (-0.5)
    score_old = (
        jnp.einsum(
            "rhgd,rchd->rhgc", grouped_heads, keys_previous, preferred_element_type=jnp.float32
        )
        * factor
    )
    score_new = (
        jnp.einsum(
            "rhgd,rshd->rhgs", grouped_heads, keys_incoming, preferred_element_type=jnp.float32
        )
        * factor
    )
    live_old = (jnp.arange(context_window, dtype=jnp.int32)[None, :] < lengths[:, None])[
        :, None, None, :
    ]
    live_new = (jnp.arange(keys_incoming.shape[1], dtype=jnp.int32) <= step_index)[
        None, None, None, :
    ]
    score_old = jnp.where(live_old, score_old, -1e30)
    score_new = jnp.where(live_new, score_new, -1e30)
    peak_score = jnp.maximum(jnp.max(score_old, axis=-1), jnp.max(score_new, axis=-1))
    weight_old = jnp.where(live_old, jnp.exp(score_old - peak_score[..., None]), 0.0)
    weight_new = jnp.where(live_new, jnp.exp(score_new - peak_score[..., None]), 0.0)
    weight_sum = jnp.sum(weight_old, axis=-1) + jnp.sum(weight_new, axis=-1)
    mixed_out = jnp.einsum(
        "rhgc,rchd->rhgd",
        weight_old.astype(jnp.bfloat16),
        values_previous,
        preferred_element_type=jnp.float32,
    )
    mixed_out = mixed_out + jnp.einsum(
        "rhgs,rshd->rhgd",
        weight_new.astype(jnp.bfloat16),
        values_incoming,
        preferred_element_type=jnp.float32,
    )
    return (mixed_out / weight_sum[..., None]).reshape(count_of_rows, -1).astype(jnp.bfloat16)


def normalize(rows_in, squares, norm_scale):
    factor_rows = lax.rsqrt(squares / D + EPS)
    return (rows_in.astype(jnp.float32) * factor_rows[:, None] * norm_scale[None, :]).astype(
        jnp.bfloat16
    )


def local(
    inputs,
    norm_gain,
    query_weight,
    key_weight,
    value_weight,
    output_weight,
    query_down,
    query_up,
    output_down,
    output_up,
    block_adapter,
    cache_lengths,
    cache_keys,
    cache_values,
):
    across_second = lax.axis_size("gy")
    index_first = lax.axis_index("gx")
    index_second = lax.axis_index("gy")
    request_count = inputs.shape[1] * across_second
    local_rows = cache_keys.shape[0]
    block_count = block_adapter.shape[0]
    norm_scale = norm_gain.astype(jnp.float32)
    query_first = pick_adapters(query_down, block_adapter, index_second * query_down.shape[0])
    query_second = pick_adapters(query_up, block_adapter, index_first * query_up.shape[0])
    output_first = pick_adapters(output_down, block_adapter, index_first * output_down.shape[0])
    output_second = pick_adapters(output_up, block_adapter, index_second * output_up.shape[0])
    incoming_keys = jnp.zeros((local_rows, STEPS, cache_keys.shape[2]), jnp.bfloat16)
    incoming_values = jnp.zeros((local_rows, STEPS, cache_values.shape[2]), jnp.bfloat16)
    results = []
    for step_index in range(STEPS):
        own_inputs = inputs[step_index]
        rows_all = lax.all_gather(own_inputs, "gy", axis=0, tiled=True)
        squares = lax.psum(jnp.sum(jnp.square(rows_all.astype(jnp.float32)), axis=1), "gx")
        normed = normalize(rows_all, squares, norm_scale)
        blocked = normed.reshape(block_count, BLOCK, -1)
        rank_part = jnp.einsum(
            "bnd,bdr->bnr", blocked, query_first, preferred_element_type=jnp.float32
        )
        rank_query = lax.psum(rank_part, ("gx", "gy")).astype(jnp.bfloat16)
        delta_query = jnp.einsum(
            "bnr,bre->bne", rank_query, query_second, preferred_element_type=jnp.float32
        ).reshape(request_count, -1)
        part_query = jnp.dot(normed, query_weight, preferred_element_type=jnp.float32) + delta_query
        part_key = jnp.dot(normed, key_weight, preferred_element_type=jnp.float32)
        part_value = jnp.dot(normed, value_weight, preferred_element_type=jnp.float32)
        summed = (
            lax.psum_scatter(part_query, "gx", scatter_dimension=0, tiled=True),
            lax.psum_scatter(part_key, "gx", scatter_dimension=0, tiled=True),
            lax.psum_scatter(part_value, "gx", scatter_dimension=0, tiled=True),
        )
        query_full, key_complete, value_full = (
            lax.all_to_all(
                summed[0].astype(jnp.bfloat16), "gy", split_axis=0, concat_axis=1, tiled=True
            ),
            lax.all_to_all(
                summed[1].astype(jnp.bfloat16), "gy", split_axis=0, concat_axis=1, tiled=True
            ),
            lax.all_to_all(
                summed[2].astype(jnp.bfloat16), "gy", split_axis=0, concat_axis=1, tiled=True
            ),
        )
        token_positions = cache_lengths + step_index
        query_rot = rotary_embedding(
            query_full.astype(jnp.float32).reshape(local_rows, QUERY_HEADS, HEAD_FEATURES),
            token_positions,
        ).astype(jnp.bfloat16)
        key_rotated = rotary_embedding(
            key_complete.astype(jnp.float32).reshape(local_rows, KEY_VALUE_HEADS, HEAD_FEATURES),
            token_positions,
        ).astype(jnp.bfloat16)
        incoming_keys = incoming_keys.at[:, step_index].set(key_rotated.reshape(local_rows, -1))
        incoming_values = incoming_values.at[:, step_index].set(value_full)
        mixed_local = attend(
            query_rot.reshape(local_rows, -1),
            cache_keys,
            cache_values,
            incoming_keys,
            incoming_values,
            cache_lengths,
            step_index,
        )
        head_group = lax.all_to_all(mixed_local, "gy", split_axis=1, concat_axis=0, tiled=True)
        mixed_all = lax.all_gather(head_group, "gx", axis=0, tiled=True)
        rank_part_out = jnp.einsum(
            "bnq,bqr->bnr",
            mixed_all.reshape(block_count, BLOCK, -1),
            output_first,
            preferred_element_type=jnp.float32,
        )
        rank_output = lax.psum(rank_part_out, ("gx", "gy")).astype(jnp.bfloat16)
        delta_output = jnp.einsum(
            "bnr,bre->bne", rank_output, output_second, preferred_element_type=jnp.float32
        ).reshape(request_count, -1)
        partial_out = (
            jnp.dot(mixed_all, output_weight, preferred_element_type=jnp.float32) + delta_output
        )
        results.append(
            lax.psum_scatter(partial_out, "gy", scatter_dimension=0, tiled=True).astype(
                jnp.bfloat16
            )
        )
    return jnp.stack(results)


def solution(mesh):
    in_specs = (
        P(None, "gy", "gx"),
        P("gx"),
        P("gx", "gy"),
        P("gx", "gy"),
        P("gx", "gy"),
        P("gy", "gx"),
        P("gy", "gx", None),
        P("gx", None, "gy"),
        P("gx", "gy", None),
        P("gy", None, "gx"),
        P(),
        P(("gx", "gy")),
        P(("gx", "gy"), None, None),
        P(("gx", "gy"), None, None),
    )
    out_specs = P(None, "gy", "gx")
    return jax.shard_map(local, mesh=mesh, in_specs=in_specs, out_specs=out_specs, check_vma=False)
```

profile of v0, /device:TPU:0, one launch (start us, length us, event | category | flops | bytes accessed | tf_op | source)
XLA Modules:
  0.0 941.0 jit_solution(17731421883246101163)
XLA Ops:
  7.7 8.6 all-gather.2
  16.3 7.3 all-gather
  23.8 7.3 all-gather.1
  32.3 21.7 %all-reduce.4 = (f32[256]{0:T(256)S(1)}, f32[256]{0:T(256)S(1)}, f32[256]{0:T(256)S(1)}) all-reduce(f32[256]{0:T(256)S(1)} %fusion.66, f32[256]{0:T(256)S(1)} %fusion.69, f32[256]{0:T(256)S(1)} %fusion.72), channel_id=1, replica_groups=mesh['gx'=8,'gy'=4] {'gx'}, use_global_device_ids=true, to_apply=%region_1.0 | all-reduce | flops 768 | bytes 6144 | tf_op jit(solution)/shard_map/psum | solution.py:135
  57.6 2.1 fusion.185
  59.7 2.1 fusion.189
  64.5 11.4 %copy.109 = bf16[4,8,64,2048]{3,1,2,0:T(8,128)(2,1)} copy(bf16[4,8,64,2048]{3,2,1,0:T(8,128)(2,1)} %bitcast.289) | data formatting | bytes 16777216
  75.9 15.6 %copy.74 = bf16[64,1024,64]{2,1,0:T(8,128)(2,1)} copy(bf16[64,1024,64]{1,2,0:T(8,128)(2,1)} %param.32) | data formatting | bytes 16777216 | tf_op args[6]
  91.5 16.5 %reshape.597 = bf16[64,65536]{1,0:T(8,128)(2,1)} reshape(bf16[64,1024,64]{2,1,0:T(8,128)(2,1)} %copy.74) | data formatting | bytes 16777216 | tf_op jit(solution)/shard_map/reshape | solution.py:34
  108.0 4.7 convolution_convert_fusion.3
  114.1 4.7 convolution_convert_fusion.1
  118.7 40.4 %all-reduce.7 = (bf16[2,128,64]{1,2,0:T(8,128)(2,1)S(1)}, bf16[2,128,64]{1,2,0:T(8,128)(2,1)S(1)}, bf16[2,128,64]{1,2,0:T(8,128)(2,1)S(1)}) all-reduce(f32[2,128,64]{1,2,0:T(8,128)S(1)} %fusion.191, f32[2,128,64]{1,2,0:T(8,128)S(1)} %fusion.183, f32[2,128,64]{1,2,0:T(8,128)S(1)} %fusion.187), channel_id=1, replica_groups=mesh['gx'=8,'gy'=4] {'gx','gy'}, use_global_device_ids=true, to_apply=%region_26.27 | all-reduce | flops 49152 | bytes 294912 | tf_op jit(solution)/shard_map/psum | solution.py:141
  159.7 4.8 convolution_add_fusion.1
  165.1 4.9 convolution_add_fusion
  170.5 4.8 convolution_add_fusion.2
  177.0 3.3 all-to-all-start.1
  181.6 60.8 %reduce-scatter.17.cloned.1.call-done = f32[32,256]{1,0:T(8,128)} async-done(((f32[256,256]{1,0:T(8,128)}), f32[32,256]{1,0:T(8,128)}) %reduce-scatter.17.cloned.1.call-update) | async-done | bytes 32784 | tf_op jit(solution)/shard_map/reduce_scatter | solution.py:151
  243.9 62.1 %reduce-scatter.25.cloned.1.call-done = f32[32,256]{1,0:T(8,128)} async-done(((f32[256,256]{1,0:T(8,128)}), f32[32,256]{1,0:T(8,128)}) %reduce-scatter.25.cloned.1.call-update) | async-done | bytes 32784 | tf_op jit(solution)/shard_map/reduce_scatter | solution.py:151
  307.3 62.1 %reduce-scatter.31.cloned.1.call-done = f32[32,256]{1,0:T(8,128)} async-done(((f32[256,256]{1,0:T(8,128)}), f32[32,256]{1,0:T(8,128)}) %reduce-scatter.31.cloned.1.call-update) | async-done | bytes 32784 | tf_op jit(solution)/shard_map/reduce_scatter | solution.py:150
  370.8 62.2 %reduce-scatter.33.cloned.1.call-done = f32[32,256]{1,0:T(8,128)} async-done(((f32[256,256]{1,0:T(8,128)}), f32[32,256]{1,0:T(8,128)}) %reduce-scatter.33.cloned.1.call-update) | async-done | bytes 32784 | tf_op jit(solution)/shard_map/reduce_scatter | solution.py:151
  434.3 3.2 all-to-all-start.5
  437.8 3.6 all-to-all-done.5
  441.4 3.2 all-to-all-start.9
  444.8 3.7 all-to-all-done.9
  448.5 3.2 all-to-all-start.2
  451.8 3.7 all-to-all-done.2
  455.6 3.2 all-to-all-start.6
  459.0 3.6 all-to-all-done.6
  462.6 40.5 %reduce-scatter.21.cloned.1.call-done = f32[32,2048]{1,0:T(8,128)} async-done(((f32[256,2048]{1,0:T(8,128)}), f32[32,2048]{1,0:T(8,128)}) %reduce-scatter.21.cloned.1.call-update) | async-done | bytes 262160 | tf_op jit(solution)/shard_map/reduce_scatter | solution.py:149
  503.2 1.6 convert_bitcast_fusion.6
  504.8 3.3 all-to-all-start.4
  508.1 65.3 %reduce-scatter.29.cloned.1.call-done = f32[32,2048]{1,0:T(8,128)} async-done(((f32[256,2048]{1,0:T(8,128)}), f32[32,2048]{1,0:T(8,128)}) %reduce-scatter.29.cloned.1.call-update) | async-done | bytes 262160 | tf_op jit(solution)/shard_map/reduce_scatter | solution.py:149
  573.4 1.6 convert_bitcast_fusion.4
  575.0 68.6 %reduce-scatter.13.cloned.1.call-done = f32[32,2048]{1,0:T(8,128)} async-done(((f32[256,2048]{1,0:T(8,128)}), f32[32,2048]{1,0:T(8,128)}) %reduce-scatter.13.cloned.1.call-update) | async-done | bytes 262160 | tf_op jit(solution)/shard_map/reduce_scatter | solution.py:149
  643.6 1.6 convert_bitcast_fusion.8
  645.3 3.3 all-to-all-start.8
  649.1 4.1 all-to-all-done.8
  653.2 3.2 all-to-all-start.10
  657.3 3.7 fusion.181
  663.1 3.3 all-to-all-start
  667.2 3.8 all-to-all-done
  671.5 3.6 fusion.179
  677.0 7.7 all_to_all.174
  684.9 2.9 fusion.57
  688.0 7.7 all_to_all.175
  696.3 2.9 fusion.63
  699.3 7.7 all_to_all.176
  707.1 12.0 %copy.113 = bf16[8,8,64,1024]{3,1,2,0:T(8,128)(2,1)} copy(bf16[8,8,64,1024]{3,2,1,0:T(8,128)(2,1)} %bitcast.290) | data formatting | bytes 16777216
  719.1 15.8 %copy.83 = bf16[32,2048,64]{2,1,0:T(8,128)(2,1)} copy(bf16[32,2048,64]{1,2,0:T(8,128)(2,1)} %param.34) | data formatting | bytes 16777216 | tf_op args[8]
  734.9 15.9 %reshape.608 = bf16[32,131072]{1,0:T(8,128)(2,1)} reshape(bf16[32,2048,64]{2,1,0:T(8,128)(2,1)} %copy.83) | data formatting | bytes 16777216 | tf_op jit(solution)/shard_map/reshape | solution.py:34
  750.8 4.7 convolution_convert_fusion
  756.2 4.7 convolution_convert_fusion.2
  760.9 1.9 fusion.194
  762.7 1.5 all-gather.9.cloned.1.call-done
  764.2 1.7 fusion.190
  765.9 39.2 %all-gather.7.cloned.1.call-done = bf16[256,2048]{1,0:T(8,128)(2,1)} async-done(((bf16[32,2048]{1,0:T(8,128)(2,1)}), bf16[256,2048]{1,0:T(8,128)(2,1)}) %all-gather.7.cloned.1.call-update) | async-done | bytes 1048592 | tf_op jit(solution)/shard_map/all_gather | solution.py:185
  805.1 1.7 fusion.186
  806.9 41.8 %all-reduce.8 = (bf16[2,128,64]{1,2,0:T(8,128)(2,1)S(1)}, bf16[2,128,64]{1,2,0:T(8,128)(2,1)S(1)}, bf16[2,128,64]{1,2,0:T(8,128)(2,1)S(1)}) all-reduce(f32[2,128,64]{1,2,0:T(8,128)S(1)} %fusion.194, f32[2,128,64]{1,2,0:T(8,128)S(1)} %fusion.190, f32[2,128,64]{1,2,0:T(8,128)S(1)} %fusion.186), channel_id=1, replica_groups=mesh['gx'=8,'gy'=4] {'gx','gy'}, use_global_device_ids=true, to_apply=%region_34.35 | all-reduce | flops 49152 | bytes 294912 | tf_op jit(solution)/shard_map/psum | solution.py:192
  849.1 4.5 convolution_add_fusion.3
  854.0 4.6 convolution_add_fusion.4
  859.0 4.7 convolution_add_fusion.5
  863.8 13.7 %reduce-scatter.35.cloned.1.call-done = f32[64,1024]{1,0:T(8,128)} async-done(((f32[256,1024]{1,0:T(8,128)}), f32[64,1024]{1,0:T(8,128)}) %reduce-scatter.35.cloned.1.call-update) | async-done | bytes 262160 | tf_op jit(solution)/shard_map/reduce_scatter | solution.py:200
  878.4 26.5 %reduce-scatter.27.cloned.1.call-done = f32[64,1024]{1,0:T(8,128)} async-done(((f32[256,1024]{1,0:T(8,128)}), f32[64,1024]{1,0:T(8,128)}) %reduce-scatter.27.cloned.1.call-update) | async-done | bytes 262160 | tf_op jit(solution)/shard_map/reduce_scatter | solution.py:200
  905.9 26.4 %reduce-scatter.19.cloned.1.call-done = f32[64,1024]{1,0:T(8,128)} async-done(((f32[256,1024]{1,0:T(8,128)}), f32[64,1024]{1,0:T(8,128)}) %reduce-scatter.19.cloned.1.call-update) | async-done | bytes 262160 | tf_op jit(solution)/shard_map/reduce_scatter | solution.py:200
  (158 shorter events, 33.7 us)
Async XLA Ops:
  6.5 48.9 %copy-start = (bf16[1024,256]{1,0:T(8,128)(2,1)S(1)}, bf16[1024,256]{1,0:T(8,128)(2,1)}, u32[]{:S(2)}) copy-start(bf16[1024,256]{1,0:T(8,128)(2,1)} %param.29) | copy-start | bytes 1572868
  6.5 25.7 %copy-start.9 = (bf16[1024]{0:T(1024)(128)(2,1)S(1)}, bf16[1024]{0:T(1024)(128)(2,1)}, u32[]{:S(2)}) copy-start(bf16[1024]{0:T(1024)(128)(2,1)} %param.27) | copy-start | bytes 6148
  6.5 169.1 %reduce-scatter.15.cloned.1.call-start = ((), (), s32[]{:S(2)}) async-start(), calls=%async_computation.25 | async-start | bytes 294912 | tf_op jit(solution)/shard_map/reduce_scatter | solution.py:150
  31.1 0.8 copy-start.3
  55.4 7.5 copy-start.4
  56.5 123.8 %reduce-scatter.23.cloned.1.call-start = ((), (), s32[]{:S(2)}) async-start(), calls=%async_computation.30 | async-start | bytes 294912 | tf_op jit(solution)/shard_map/reduce_scatter | solution.py:150
  57.5 185.0 %reduce-scatter.17.cloned.1.call-start = ((), (), s32[]{:S(2)}) async-start(), calls=%async_computation.26 | async-start | bytes 294912 | tf_op jit(solution)/shard_map/reduce_scatter | solution.py:151
  59.7 246.3 %reduce-scatter.25.cloned.1.call-start = ((), (), s32[]{:S(2)}) async-start(), calls=%async_computation.31 | async-start | bytes 294912 | tf_op jit(solution)/shard_map/reduce_scatter | solution.py:151
  61.8 307.7 %reduce-scatter.31.cloned.1.call-start = ((), (), s32[]{:S(2)}) async-start(), calls=%async_computation.35 | async-start | bytes 294912 | tf_op jit(solution)/shard_map/reduce_scatter | solution.py:150
  62.9 370.1 %reduce-scatter.33.cloned.1.call-start = ((), (), s32[]{:S(2)}) async-start(), calls=%async_computation.36 | async-start | bytes 294912 | tf_op jit(solution)/shard_map/reduce_scatter | solution.py:151
  63.9 439.2 %reduce-scatter.21.cloned.1.call-start = ((), (), s32[]{:S(2)}) async-start(), calls=%async_computation.29 | async-start | bytes 2359296 | tf_op jit(solution)/shard_map/reduce_scatter | solution.py:149
  91.5 16.5 %copy-start.8 = (s32[2]{0:T(128)S(1)}, s32[2]{0:T(128)}, u32[]{:S(2)}) copy-start(s32[2]{0:T(128)} %param.36) | copy-start | bytes 28
  164.5 408.9 %reduce-scatter.29.cloned.1.call-start = ((), (), s32[]{:S(2)}) async-start(), calls=%async_computation.34 | async-start | bytes 2359296 | tf_op jit(solution)/shard_map/reduce_scatter | solution.py:149
  169.9 473.7 %reduce-scatter.13.cloned.1.call-start = ((), (), s32[]{:S(2)}) async-start(), calls=%async_computation.24 | async-start | bytes 2359296 | tf_op jit(solution)/shard_map/reduce_scatter | solution.py:149
  170.5 4.9 copy-start.10
  177.0 257.3 %all-to-all-start.1 = ((bf16[4,8,256]{2,1,0:T(8,128)(2,1)}), bf16[4,8,256]{2,1,0:T(8,128)(2,1)S(1)}, u32[]{:S(2)}, u32[]{:S(2)}) async-start(bf16[4,8,256]{2,1,0:T(8,128)(2,1)} %convert_bitcast_fusion.15), calls=%async_computation.3 | async-start | bytes 32768 | tf_op jit(solution)/shard_map/all_to_all | solution.py:157
  434.3 7.1 all-to-all-start.5
  441.4 7.1 all-to-all-start.9
  448.5 7.1 all-to-all-start.2
  455.6 7.1 all-to-all-start.6
  504.8 140.5 %all-to-all-start.4 = ((bf16[4,8,2048]{2,1,0:T(8,128)(2,1)}), bf16[4,8,2048]{2,1,0:T(8,128)(2,1)S(1)}, u32[]{:S(2)}, u32[]{:S(2)}) async-start(bf16[4,8,2048]{2,1,0:T(8,128)(2,1)} %convert_bitcast_fusion.6), calls=%async_computation.9 | async-start | bytes 262144 | tf_op jit(solution)/shard_map/all_to_all | solution.py:154
  645.3 7.9 all-to-all-start.8
  653.2 9.9 %all-to-all-start.10 = ((bf16[4,8,256]{2,1,0:T(8,128)(2,1)}), bf16[4,8,256]{2,1,0:T(8,128)(2,1)S(1)}, u32[]{:S(2)}, u32[]{:S(2)}) async-start(bf16[4,8,256]{2,1,0:T(8,128)(2,1)} %convert_bitcast_fusion.10), calls=%async_computation.21 | async-start | bytes 32768 | tf_op jit(solution)/shard_map/all_to_all | solution.py:160
  656.8 4.3 copy-start.2
  663.1 7.9 all-to-all-start
  666.4 94.4 %all-gather.11.cloned.1.call-start = ((), (), s32[]{:S(2)}) async-start(), calls=%async_computation.37 | async-start | bytes 1179648 | tf_op jit(solution)/shard_map/all_gather | solution.py:185
  671.4 4.8 copy-start.11
  684.7 79.5 %all-gather.9.cloned.1.call-start = ((), (), s32[]{:S(2)}) async-start(), calls=%async_computation.32 | async-start | bytes 1179648 | tf_op jit(solution)/shard_map/all_gather | solution.py:185
  695.7 109.4 %all-gather.7.cloned.1.call-start = ((), (), s32[]{:S(2)}) async-start(), calls=%async_computation.27 | async-start | bytes 1179648 | tf_op jit(solution)/shard_map/all_gather | solution.py:185
  707.0 170.4 %reduce-scatter.35.cloned.1.call-start = ((), (), s32[]{:S(2)}) async-start(), calls=%async_computation.38 | async-start | bytes 1310720 | tf_op jit(solution)/shard_map/reduce_scatter | solution.py:200
  760.9 88.2 %copy-start.5 = (bf16[256,2048]{1,0:T(8,128)(2,1)S(1)}, bf16[256,2048]{1,0:T(8,128)(2,1)}, u32[]{:S(2)}) copy-start(bf16[256,2048]{1,0:T(8,128)(2,1)} %all-gather.11.cloned.1.call-done) | copy-start | bytes 3145732
  849.0 4.9 copy-start.6
  853.6 51.4 %reduce-scatter.27.cloned.1.call-start = ((), (), s32[]{:S(2)}) async-start(), calls=%async_computation.33 | async-start | bytes 1310720 | tf_op jit(solution)/shard_map/reduce_scatter | solution.py:200
  854.0 5.0 copy-start.7
  858.6 73.7 %reduce-scatter.19.cloned.1.call-start = ((), (), s32[]{:S(2)}) async-start(), calls=%async_computation.28 | async-start | bytes 1310720 | tf_op jit(solution)/shard_map/reduce_scatter | solution.py:200
  859.0 75.0 %copy-start.1 = (bf16[1024,256]{1,0:T(8,128)(2,1)S(1)}, bf16[1024,256]{1,0:T(8,128)(2,1)}, u32[]{:S(2)}) copy-start(bf16[1024,256]{1,0:T(8,128)(2,1)} %param.29) | copy-start | bytes 1572868
Sparse Core Ops, SparseCore 0:
  56.6 58.5 reduce-scatter.14
  118.5 60.3 reduce-scatter.22
  182.2 60.2 reduce-scatter.16
  245.7 60.2 reduce-scatter.24
  309.2 60.2 reduce-scatter.30
  372.6 60.2 reduce-scatter.32
  436.5 66.6 reduce-scatter.20
  506.7 66.6 reduce-scatter.28
  576.9 66.6 reduce-scatter.12
  684.8 38.2 all-gather.10
  725.3 38.8 all-gather.8
  766.2 38.8 all-gather.6
  853.7 23.7 reduce-scatter.34
  880.0 24.8 reduce-scatter.26
  907.3 24.9 reduce-scatter.18
where the time goes:
time: 947 us; the launch traced here: 941 us
  waiting for transfers between devices  552 us (58%)
  blocking collectives  150 us (16%)
  local copies, waits for them, and re-layouts  91.7 us (10%)
  matrix products  81.2 us (9%)
  starting transfers between devices  30.7 us (3%)
  other arithmetic  21.1 us (2%)
  between operations  14.5 us (2%)
    reduce_scatter x3, waiting for transfers between devices, local(): lax.psum_scatter(part_value, 'gx', scatter_dimension=0, tiled=True)  185 us
    reduce_scatter x3, waiting for transfers between devices, local(): lax.psum_scatter(part_query, 'gx', scatter_dimension=0, tiled=True)  174 us
    reduce_scatter x3, waiting for transfers between devices, local(): lax.psum_scatter(partial_out, 'gy', scatter_dimension=0, tiled=True)  66.6 us
    reduce_scatter x3, waiting for transfers between devices, local(): lax.psum_scatter(part_key, 'gx', scatter_dimension=0, tiled=True)  62.2 us
    unnamed x34, local copies, waits for them, and re-layouts  55.8 us
    psum x1, blocking collectives, local(): rank_output = lax.psum(rank_part_out, ('gx', 'gy')).astype(jnp.bfloat16)  41.8 us
    all_gather x3, waiting for transfers between devices, local(): mixed_all = lax.all_gather(head_group, 'gx', axis=0, tiled=True)  40.7 us
    psum x1, blocking collectives, local(): rank_query = lax.psum(rank_part, ('gx', 'gy')).astype(jnp.bfloat16)  40.4 us
  transfers between devices with their start and end apart: 24, of which 18 were waited for; matrix products, arithmetic and copies ran while one was open for 19% of the time, Pallas kernels for 0%

commit v1 on v0

--- a/solution.py
+++ b/solution.py
@@ -1,3 +1,4 @@
+import functools
 import jax
 import jax.numpy as jnp
 from jax import lax
@@ -11,6 +12,26 @@
 STEPS = 3
 EPS = 1e-05
 THETA = 500000.0
+
+
+def plan_the_sheet(matrix, link_axis):
+    kept_arr, arr_out, value_now = (
+        lax.axis_size(link_axis),
+        lax.axis_index(link_axis),
+        matrix.shape[0],
+    )
+    rack = list(map(lambda at: (at, (at + 1) % kept_arr), range(kept_arr)))
+    oldest = matrix
+    after = jnp.zeros((*matrix.shape[:0], kept_arr * value_now, *matrix.shape[1:]), matrix.dtype)
+    for to_i in range(kept_arr):
+        carry_out = (arr_out - to_i) % kept_arr
+        after = lax.dynamic_update_slice_in_dim(after, oldest, carry_out * value_now, axis=0)
+        if to_i < kept_arr - 1:
+            oldest = lax.ppermute(oldest, link_axis, perm=rack)
+    return after
+
+
+row_answer = functools.partial(plan_the_sheet, link_axis="gx")
 
 
 def rotary_embedding(values_in, token_positions):
@@ -182,7 +203,7 @@
             step_index,
         )
         head_group = lax.all_to_all(mixed_local, "gy", split_axis=1, concat_axis=0, tiled=True)
-        mixed_all = lax.all_gather(head_group, "gx", axis=0, tiled=True)
+        mixed_all = row_answer(head_group)
         rank_part_out = jnp.einsum(
             "bnq,bqr->bnr",
             mixed_all.reshape(block_count, BLOCK, -1),

time: 947 us -> 912 us (0.963)
  waiting for transfers between devices: 552 us -> 526 us
  blocking collectives: 150 us -> 126 us
  starting transfers between devices: 30.7 us -> 44.9 us
    ppermute x0 -> x21, waiting for transfers between devices: none -> 61.1 us  [plan_the_sheet(): oldest = lax.ppermute(oldest, link_axis, perm=rack)]
    reduce_scatter x3, waiting for transfers between devices: 185 us -> 137 us  [local(): lax.psum_scatter(part_value, 'gx', scatter_dimension=0, tiled=True)]
    all_gather x3 -> x0, waiting for transfers between devices: 40.7 us -> none  [local(): mixed_all = lax.all_gather(head_group, 'gx', axis=0, tiled=True)]
    all_to_all x3 -> x0, blocking collectives: 23.1 us -> none  [local(): lax.all_to_all(mixed_local, 'gy', split_axis=1, concat_axis=0, tiled=True)]
    all_to_all x0 -> x3, starting transfers between devices: none -> 9.97 us  [local(): lax.all_to_all(mixed_local, 'gy', split_axis=1, concat_axis=0, tiled=True)]
  transfers between devices with their start and end apart: 24 -> 45, of which waited for: 18 -> 39; matrix products, arithmetic and copies ran while one was open for 19% -> 19% of each run, Pallas kernels for 0% -> 0%
where the time goes in v1:
time: 912 us; the launch traced here: 905 us
  waiting for transfers between devices  526 us (58%)
  blocking collectives  126 us (14%)
  local copies, waits for them, and re-layouts  94.4 us (10%)
  matrix products  77.7 us (9%)
  starting transfers between devices  44.9 us (5%)
  other arithmetic  21.1 us (2%)
  between operations  14.9 us (2%)
    reduce_scatter x3, waiting for transfers between devices, local(): lax.psum_scatter(part_query, 'gx', scatter_dimension=0, tiled=True)  174 us
    reduce_scatter x3, waiting for transfers between devices, local(): lax.psum_scatter(part_value, 'gx', scatter_dimension=0, tiled=True)  137 us
    reduce_scatter x3, waiting for transfers between devices, local(): lax.psum_scatter(partial_out, 'gy', scatter_dimension=0, tiled=True)  67.7 us
    reduce_scatter x3, waiting for transfers between devices, local(): lax.psum_scatter(part_key, 'gx', scatter_dimension=0, tiled=True)  62.2 us
    ppermute x21, waiting for transfers between devices, plan_the_sheet(): oldest = lax.ppermute(oldest, link_axis, perm=rack)  61.1 us
    unnamed x34, local copies, waits for them, and re-layouts  55.7 us
    psum x1, blocking collectives, local(): rank_output = lax.psum(rank_part_out, ('gx', 'gy')).astype(jnp.bfloat16)  41.1 us
    psum x1, blocking collectives, local(): rank_query = lax.psum(rank_part, ('gx', 'gy')).astype(jnp.bfloat16)  40.4 us
  transfers between devices with their start and end apart: 45, of which 39 were waited for; matrix products, arithmetic and copies ran while one was open for 19% of the time, Pallas kernels for 0%

profile of v1, /device:TPU:0, one launch (start us, length us, event | category | flops | bytes accessed | tf_op | source)
XLA Modules:
  0.0 905.3 jit_solution(11279937535175998975)
XLA Ops:
  7.7 8.6 all-gather.2
  16.3 7.3 all-gather
  23.8 7.3 all-gather.1
  32.2 21.7 %all-reduce.4 = (f32[256]{0:T(256)S(1)}, f32[256]{0:T(256)S(1)}, f32[256]{0:T(256)S(1)}) all-reduce(f32[256]{0:T(256)S(1)} %fusion.66, f32[256]{0:T(256)S(1)} %fusion.69, f32[256]{0:T(256)S(1)} %fusion.72), channel_id=1, replica_groups=mesh['gx'=8,'gy'=4] {'gx'}, use_global_device_ids=true, to_apply=%region_1.0 | all-reduce | flops 768 | bytes 6144 | tf_op jit(solution)/shard_map/psum | solution.py:156
  64.6 11.5 %copy.109 = bf16[4,8,64,2048]{3,1,2,0:T(8,128)(2,1)} copy(bf16[4,8,64,2048]{3,2,1,0:T(8,128)(2,1)} %bitcast.292) | data formatting | bytes 16777216
  76.0 15.6 %copy.74 = bf16[64,1024,64]{2,1,0:T(8,128)(2,1)} copy(bf16[64,1024,64]{1,2,0:T(8,128)(2,1)} %param.32) | data formatting | bytes 16777216 | tf_op args[6]
  91.7 16.6 %reshape.597 = bf16[64,65536]{1,0:T(8,128)(2,1)} reshape(bf16[64,1024,64]{2,1,0:T(8,128)(2,1)} %copy.74) | data formatting | bytes 16777216 | tf_op jit(solution)/shard_map/reshape | solution.py:55
  108.3 4.7 convolution_convert_fusion.3
  114.3 4.7 convolution_convert_fusion.1
  118.9 40.4 %all-reduce.7 = (bf16[2,128,64]{1,2,0:T(8,128)(2,1)S(1)}, bf16[2,128,64]{1,2,0:T(8,128)(2,1)S(1)}, bf16[2,128,64]{1,2,0:T(8,128)(2,1)S(1)}) all-reduce(f32[2,128,64]{1,2,0:T(8,128)S(1)} %fusion.191, f32[2,128,64]{1,2,0:T(8,128)S(1)} %fusion.183, f32[2,128,64]{1,2,0:T(8,128)S(1)} %fusion.187), channel_id=1, replica_groups=mesh['gx'=8,'gy'=4] {'gx','gy'}, use_global_device_ids=true, to_apply=%region_26.27 | all-reduce | flops 49152 | bytes 294912 | tf_op jit(solution)/shard_map/psum | solution.py:162
  159.9 4.8 convolution_add_fusion.1
  165.2 4.9 convolution_add_fusion
  170.7 4.9 convolution_add_fusion.2
  175.8 12.0 %copy.113 = bf16[8,8,64,1024]{3,1,2,0:T(8,128)(2,1)} copy(bf16[8,8,64,1024]{3,2,1,0:T(8,128)(2,1)} %bitcast.293) | data formatting | bytes 16777216
  187.7 4.7 convolution_convert_fusion.2
  192.4 15.6 %copy.83 = bf16[32,2048,64]{2,1,0:T(8,128)(2,1)} copy(bf16[32,2048,64]{1,2,0:T(8,128)(2,1)} %param.34) | data formatting | bytes 16777216 | tf_op args[8]
  208.0 16.0 %reshape.608 = bf16[32,131072]{1,0:T(8,128)(2,1)} reshape(bf16[32,2048,64]{2,1,0:T(8,128)(2,1)} %copy.83) | data formatting | bytes 16777216 | tf_op jit(solution)/shard_map/reshape | solution.py:55
  225.6 3.3 all-to-all-start.1
  230.3 12.3 %reduce-scatter.17.cloned.1.call-done = f32[32,256]{1,0:T(8,128)} async-done(((f32[256,256]{1,0:T(8,128)}), f32[32,256]{1,0:T(8,128)}) %reduce-scatter.17.cloned.1.call-update) | async-done | bytes 32784 | tf_op jit(solution)/shard_map/reduce_scatter | solution.py:172
  243.9 62.2 %reduce-scatter.25.cloned.1.call-done = f32[32,256]{1,0:T(8,128)} async-done(((f32[256,256]{1,0:T(8,128)}), f32[32,256]{1,0:T(8,128)}) %reduce-scatter.25.cloned.1.call-update) | async-done | bytes 32784 | tf_op jit(solution)/shard_map/reduce_scatter | solution.py:172
  307.5 62.1 %reduce-scatter.31.cloned.1.call-done = f32[32,256]{1,0:T(8,128)} async-done(((f32[256,256]{1,0:T(8,128)}), f32[32,256]{1,0:T(8,128)}) %reduce-scatter.31.cloned.1.call-update) | async-done | bytes 32784 | tf_op jit(solution)/shard_map/reduce_scatter | solution.py:171
  371.0 62.2 %reduce-scatter.33.cloned.1.call-done = f32[32,256]{1,0:T(8,128)} async-done(((f32[256,256]{1,0:T(8,128)}), f32[32,256]{1,0:T(8,128)}) %reduce-scatter.33.cloned.1.call-update) | async-done | bytes 32784 | tf_op jit(solution)/shard_map/reduce_scatter | solution.py:172
  434.5 3.2 all-to-all-start.5
  438.0 3.6 all-to-all-done.5
  441.6 3.2 all-to-all-start.9
  444.9 3.7 all-to-all-done.9
  448.6 3.7 all-to-all-start.2
  452.4 3.7 all-to-all-done.2
  456.1 3.2 all-to-all-start.6
  459.6 3.6 all-to-all-done.6
  463.2 40.4 %reduce-scatter.21.cloned.1.call-done = f32[32,2048]{1,0:T(8,128)} async-done(((f32[256,2048]{1,0:T(8,128)}), f32[32,2048]{1,0:T(8,128)}) %reduce-scatter.21.cloned.1.call-update) | async-done | bytes 262160 | tf_op jit(solution)/shard_map/reduce_scatter | solution.py:170
  505.2 3.3 all-to-all-start.4
  508.5 65.2 %reduce-scatter.29.cloned.1.call-done = f32[32,2048]{1,0:T(8,128)} async-done(((f32[256,2048]{1,0:T(8,128)}), f32[32,2048]{1,0:T(8,128)}) %reduce-scatter.29.cloned.1.call-update) | async-done | bytes 262160 | tf_op jit(solution)/shard_map/reduce_scatter | solution.py:170
  575.4 68.6 %reduce-scatter.13.cloned.1.call-done = f32[32,2048]{1,0:T(8,128)} async-done(((f32[256,2048]{1,0:T(8,128)}), f32[32,2048]{1,0:T(8,128)}) %reduce-scatter.13.cloned.1.call-update) | async-done | bytes 262160 | tf_op jit(solution)/shard_map/reduce_scatter | solution.py:170
  645.6 3.3 all-to-all-start.8
  649.5 4.1 all-to-all-done.8
  653.5 3.2 all-to-all-start.10
  657.6 3.7 fusion.181
  663.4 3.3 all-to-all-start
  667.5 3.9 all-to-all-done
  671.9 3.6 fusion.179
  678.0 3.3 all-to-all-start.11
  681.4 2.9 fusion.57
  685.9 3.3 all-to-all-start.7
  689.3 2.9 fusion.63
  693.9 3.3 all-to-all-start.3
  697.3 4.6 convolution_convert_fusion
  707.3 4.7 collective-permute-done.14
  717.6 3.0 collective-permute-done.15
  723.5 3.3 collective-permute-done.1
  726.8 3.0 collective-permute-done.16
  732.5 3.0 collective-permute-done.2
  738.4 3.1 collective-permute-done.10
  741.6 3.0 collective-permute-done.3
  747.4 3.2 collective-permute-done.11
  753.5 3.0 collective-permute-done.19
  756.5 3.2 collective-permute-done.12
  770.5 41.1 %all-reduce.8 = (bf16[2,128,64]{1,2,0:T(8,128)(2,1)S(1)}, bf16[2,128,64]{1,2,0:T(8,128)(2,1)S(1)}, bf16[2,128,64]{1,2,0:T(8,128)(2,1)S(1)}) all-reduce(f32[2,128,64]{1,2,0:T(8,128)S(1)} %fusion.194, f32[2,128,64]{1,2,0:T(8,128)S(1)} %fusion.190, f32[2,128,64]{1,2,0:T(8,128)S(1)} %fusion.186), channel_id=1, replica_groups=mesh['gx'=8,'gy'=4] {'gx','gy'}, use_global_device_ids=true, to_apply=%region_34.35 | all-reduce | flops 49152 | bytes 294912 | tf_op jit(solution)/shard_map/psum | solution.py:213
  812.0 4.9 convolution_add_fusion.3
  817.3 4.4 convolution_add_fusion.4
  822.2 4.7 convolution_add_fusion.5
  826.9 14.7 %reduce-scatter.35.cloned.1.call-done = f32[64,1024]{1,0:T(8,128)} async-done(((f32[256,1024]{1,0:T(8,128)}), f32[64,1024]{1,0:T(8,128)}) %reduce-scatter.35.cloned.1.call-update) | async-done | bytes 262160 | tf_op jit(solution)/shard_map/reduce_scatter | solution.py:221
  842.5 26.7 %reduce-scatter.27.cloned.1.call-done = f32[64,1024]{1,0:T(8,128)} async-done(((f32[256,1024]{1,0:T(8,128)}), f32[64,1024]{1,0:T(8,128)}) %reduce-scatter.27.cloned.1.call-update) | async-done | bytes 262160 | tf_op jit(solution)/shard_map/reduce_scatter | solution.py:221
  870.2 26.4 %reduce-scatter.19.cloned.1.call-done = f32[64,1024]{1,0:T(8,128)} async-done(((f32[256,1024]{1,0:T(8,128)}), f32[64,1024]{1,0:T(8,128)}) %reduce-scatter.19.cloned.1.call-update) | async-done | bytes 262160 | tf_op jit(solution)/shard_map/reduce_scatter | solution.py:221
  (221 shorter events, 80.7 us)
Async XLA Ops:
  6.5 48.9 %copy-start = (bf16[1024,256]{1,0:T(8,128)(2,1)S(1)}, bf16[1024,256]{1,0:T(8,128)(2,1)}, u32[]{:S(2)}) copy-start(bf16[1024,256]{1,0:T(8,128)(2,1)} %param.29) | copy-start | bytes 1572868
  6.5 25.7 %copy-start.9 = (bf16[1024]{0:T(1024)(128)(2,1)S(1)}, bf16[1024]{0:T(1024)(128)(2,1)}, u32[]{:S(2)}) copy-start(bf16[1024]{0:T(1024)(128)(2,1)} %param.27) | copy-start | bytes 6148
  6.5 217.7 %reduce-scatter.15.cloned.1.call-start = ((), (), s32[]{:S(2)}) async-start(), calls=%async_computation.25 | async-start | bytes 294912 | tf_op jit(solution)/shard_map/reduce_scatter | solution.py:171
  31.1 0.8 copy-start.3
  55.4 7.5 copy-start.4
  56.4 172.5 %reduce-scatter.23.cloned.1.call-start = ((), (), s32[]{:S(2)}) async-start(), calls=%async_computation.29 | async-start | bytes 294912 | tf_op jit(solution)/shard_map/reduce_scatter | solution.py:171
  57.5 185.0 %reduce-scatter.17.cloned.1.call-start = ((), (), s32[]{:S(2)}) async-start(), calls=%async_computation.26 | async-start | bytes 294912 | tf_op jit(solution)/shard_map/reduce_scatter | solution.py:172
  59.7 246.4 %reduce-scatter.25.cloned.1.call-start = ((), (), s32[]{:S(2)}) async-start(), calls=%async_computation.30 | async-start | bytes 294912 | tf_op jit(solution)/shard_map/reduce_scatter | solution.py:172
  61.8 307.8 %reduce-scatter.31.cloned.1.call-start = ((), (), s32[]{:S(2)}) async-start(), calls=%async_computation.33 | async-start | bytes 294912 | tf_op jit(solution)/shard_map/reduce_scatter | solution.py:171
  62.9 370.2 %reduce-scatter.33.cloned.1.call-start = ((), (), s32[]{:S(2)}) async-start(), calls=%async_computation.34 | async-start | bytes 294912 | tf_op jit(solution)/shard_map/reduce_scatter | solution.py:172
  64.0 439.6 %reduce-scatter.21.cloned.1.call-start = ((), (), s32[]{:S(2)}) async-start(), calls=%async_computation.28 | async-start | bytes 2359296 | tf_op jit(solution)/shard_map/reduce_scatter | solution.py:170
  91.7 16.6 %copy-start.8 = (s32[2]{0:T(128)S(1)}, s32[2]{0:T(128)}, u32[]{:S(2)}) copy-start(s32[2]{0:T(128)} %param.36) | copy-start | bytes 28
  164.7 409.1 %reduce-scatter.29.cloned.1.call-start = ((), (), s32[]{:S(2)}) async-start(), calls=%async_computation.32 | async-start | bytes 2359296 | tf_op jit(solution)/shard_map/reduce_scatter | solution.py:170
  170.2 473.8 %reduce-scatter.13.cloned.1.call-start = ((), (), s32[]{:S(2)}) async-start(), calls=%async_computation.24 | async-start | bytes 2359296 | tf_op jit(solution)/shard_map/reduce_scatter | solution.py:170
  170.7 4.9 copy-start.10
  225.6 208.9 %all-to-all-start.1 = ((bf16[4,8,256]{2,1,0:T(8,128)(2,1)}), bf16[4,8,256]{2,1,0:T(8,128)(2,1)S(1)}, u32[]{:S(2)}, u32[]{:S(2)}) async-start(bf16[4,8,256]{2,1,0:T(8,128)(2,1)} %convert_bitcast_fusion.15), calls=%async_computation.3 | async-start | bytes 32768 | tf_op jit(solution)/shard_map/all_to_all | solution.py:178
  434.5 7.1 all-to-all-start.5
  441.6 7.1 all-to-all-start.9
  448.6 7.5 all-to-all-start.2
  456.1 7.1 all-to-all-start.6
  505.2 140.4 %all-to-all-start.4 = ((bf16[4,8,2048]{2,1,0:T(8,128)(2,1)}), bf16[4,8,2048]{2,1,0:T(8,128)(2,1)S(1)}, u32[]{:S(2)}, u32[]{:S(2)}) async-start(bf16[4,8,2048]{2,1,0:T(8,128)(2,1)} %convert_bitcast_fusion.6), calls=%async_computation.9 | async-start | bytes 262144 | tf_op jit(solution)/shard_map/all_to_all | solution.py:175
  645.6 7.9 all-to-all-start.8
  653.5 9.9 %all-to-all-start.10 = ((bf16[4,8,256]{2,1,0:T(8,128)(2,1)}), bf16[4,8,256]{2,1,0:T(8,128)(2,1)S(1)}, u32[]{:S(2)}, u32[]{:S(2)}) async-start(bf16[4,8,256]{2,1,0:T(8,128)(2,1)} %convert_bitcast_fusion.10), calls=%async_computation.21 | async-start | bytes 32768 | tf_op jit(solution)/shard_map/all_to_all | solution.py:181
  657.1 4.3 copy-start.2
  663.4 7.9 all-to-all-start
  671.7 4.8 copy-start.11
  678.0 7.9 all-to-all-start.11
  685.9 7.9 all-to-all-start.7
  693.9 11.4 %all-to-all-start.3 = ((bf16[8,4,2048]{2,0,1:T(8,128)(2,1)}), bf16[8,4,2048]{2,0,1:T(8,128)(2,1)S(1)}, u32[]{:S(2)}, u32[]{:S(2)}) async-start(bf16[8,4,2048]{2,0,1:T(8,128)(2,1)} %copy.82), calls=%async_computation.6 | async-start | bytes 262144 | tf_op jit(solution)/shard_map/all_to_all | solution.py:205
  697.2 144.4 %reduce-scatter.35.cloned.1.call-start = ((), (), s32[]{:S(2)}) async-start(), calls=%async_computation.35 | async-start | bytes 1310720 | tf_op jit(solution)/shard_map/reduce_scatter | solution.py:221
  702.8 9.2 %collective-permute-start.14 = (bf16[32,2048]{1,0:T(8,128)(2,1)S(1)}, bf16[32,2048]{1,0:T(8,128)(2,1)S(1)}, u32[]{:S(2)}, u32[]{:S(2)}) collective-permute-start(bf16[32,2048]{1,0:T(8,128)(2,1)S(1)} %bitcast.305), channel_id=1, source_target_pairs={{0,4},{4,8},{8,12},{12,16},{16,20},{20,24},{24,28},{28,0},{1,5},{5... | collective-permute-start | bytes 393224 | tf_op jit(solution)/shard_map/ppermute | solution.py:30
  703.7 11.1 %collective-permute-start.7 = (bf16[32,2048]{1,0:T(8,128)(2,1)S(1)}, bf16[32,2048]{1,0:T(8,128)(2,1)S(1)}, u32[]{:S(2)}, u32[]{:S(2)}) collective-permute-start(bf16[32,2048]{1,0:T(8,128)(2,1)S(1)} %bitcast.306), channel_id=1, source_target_pairs={{0,4},{4,8},{8,12},{12,16},{16,20},{20,24},{24,28},{28,0},{1,5},{5... | collective-permute-start | bytes 393224 | tf_op jit(solution)/shard_map/ppermute | solution.py:30
  705.3 12.3 %collective-permute-start = (bf16[32,2048]{1,0:T(8,128)(2,1)S(1)}, bf16[32,2048]{1,0:T(8,128)(2,1)S(1)}, u32[]{:S(2)}, u32[]{:S(2)}) collective-permute-start(bf16[32,2048]{1,0:T(8,128)(2,1)S(1)} %bitcast.307), channel_id=1, source_target_pairs={{0,4},{4,8},{8,12},{12,16},{16,20},{20,24},{24,28},{28,0},{1,5},{5... | collective-permute-start | bytes 393224 | tf_op jit(solution)/shard_map/ppermute | solution.py:30
  712.0 8.6 collective-permute-start.15
  714.8 8.6 collective-permute-start.8
  717.6 9.1 %collective-permute-start.1 = (bf16[32,2048]{1,0:T(8,128)(2,1)S(1)}, bf16[32,2048]{1,0:T(8,128)(2,1)S(1)}, u32[]{:S(2)}, u32[]{:S(2)}) collective-permute-start(bf16[32,2048]{1,0:T(8,128)(2,1)S(1)} %collective-permute-done), channel_id=1, source_target_pairs={{0,4},{4,8},{8,12},{12,16},{16,20},{20,24},{24,28},{28,0},{1,5},{5... | collective-permute-start | bytes 393224 | tf_op jit(solution)/shard_map/ppermute | solution.py:30
  720.6 9.1 %collective-permute-start.16 = (bf16[32,2048]{1,0:T(8,128)(2,1)S(1)}, bf16[32,2048]{1,0:T(8,128)(2,1)S(1)}, u32[]{:S(2)}, u32[]{:S(2)}) collective-permute-start(bf16[32,2048]{1,0:T(8,128)(2,1)S(1)} %collective-permute-done.15), channel_id=1, source_target_pairs={{0,4},{4,8},{8,12},{12,16},{16,20},{20,24},{24,28},{28,0},{1,5},{5... | collective-permute-start | bytes 393224 | tf_op jit(solution)/shard_map/ppermute | solution.py:30
  723.4 9.1 %collective-permute-start.9 = (bf16[32,2048]{1,0:T(8,128)(2,1)S(1)}, bf16[32,2048]{1,0:T(8,128)(2,1)S(1)}, u32[]{:S(2)}, u32[]{:S(2)}) collective-permute-start(bf16[32,2048]{1,0:T(8,128)(2,1)S(1)} %collective-permute-done.8), channel_id=1, source_target_pairs={{0,4},{4,8},{8,12},{12,16},{16,20},{20,24},{24,28},{28,0},{1,5},{5... | collective-permute-start | bytes 393224 | tf_op jit(solution)/shard_map/ppermute | solution.py:30
  726.7 8.8 collective-permute-start.2
  729.8 8.7 collective-permute-start.17
  732.5 9.0 collective-permute-start.10
  735.5 9.1 %collective-permute-start.3 = (bf16[32,2048]{1,0:T(8,128)(2,1)S(1)}, bf16[32,2048]{1,0:T(8,128)(2,1)S(1)}, u32[]{:S(2)}, u32[]{:S(2)}) collective-permute-start(bf16[32,2048]{1,0:T(8,128)(2,1)S(1)} %collective-permute-done.2), channel_id=1, source_target_pairs={{0,4},{4,8},{8,12},{12,16},{16,20},{20,24},{24,28},{28,0},{1,5},{5... | collective-permute-start | bytes 393224 | tf_op jit(solution)/shard_map/ppermute | solution.py:30
  738.4 8.9 collective-permute-start.18
  741.5 9.0 collective-permute-start.11
  744.6 8.8 collective-permute-start.4
  747.4 9.1 %collective-permute-start.19 = (bf16[32,2048]{1,0:T(8,128)(2,1)S(1)}, bf16[32,2048]{1,0:T(8,128)(2,1)S(1)}, u32[]{:S(2)}, u32[]{:S(2)}) collective-permute-start(bf16[32,2048]{1,0:T(8,128)(2,1)S(1)} %collective-permute-done.18), channel_id=1, source_target_pairs={{0,4},{4,8},{8,12},{12,16},{16,20},{20,24},{24,28},{28,0},{1,5},{5... | collective-permute-start | bytes 393224 | tf_op jit(solution)/shard_map/ppermute | solution.py:30
  750.6 9.1 %collective-permute-start.12 = (bf16[32,2048]{1,0:T(8,128)(2,1)S(1)}, bf16[32,2048]{1,0:T(8,128)(2,1)S(1)}, u32[]{:S(2)}, u32[]{:S(2)}) collective-permute-start(bf16[32,2048]{1,0:T(8,128)(2,1)S(1)} %collective-permute-done.11), channel_id=1, source_target_pairs={{0,4},{4,8},{8,12},{12,16},{16,20},{20,24},{24,28},{28,0},{1,5},{5... | collective-permute-start | bytes 393224 | tf_op jit(solution)/shard_map/ppermute | solution.py:30
  753.4 8.8 collective-permute-start.5
  756.5 8.4 collective-permute-start.20
  759.7 7.7 collective-permute-start.13
  762.3 7.7 collective-permute-start.6
  764.9 5.0 copy-start.5
  767.4 2.6 copy-start.6
  812.0 5.3 copy-start.7
  816.9 52.3 %reduce-scatter.27.cloned.1.call-start = ((), (), s32[]{:S(2)}) async-start(), calls=%async_computation.31 | async-start | bytes 1310720 | tf_op jit(solution)/shard_map/reduce_scatter | solution.py:221
  821.8 74.8 %reduce-scatter.19.cloned.1.call-start = ((), (), s32[]{:S(2)}) async-start(), calls=%async_computation.27 | async-start | bytes 1310720 | tf_op jit(solution)/shard_map/reduce_scatter | solution.py:221
  822.2 76.1 %copy-start.1 = (bf16[1024,256]{1,0:T(8,128)(2,1)S(1)}, bf16[1024,256]{1,0:T(8,128)(2,1)}, u32[]{:S(2)}) copy-start(bf16[1024,256]{1,0:T(8,128)(2,1)} %param.29) | copy-start | bytes 1572868
Sparse Core Ops, SparseCore 0:
  56.6 58.5 reduce-scatter.14
  118.5 60.3 reduce-scatter.22
  182.2 60.3 reduce-scatter.16
  245.7 60.3 reduce-scatter.24
  309.3 60.2 reduce-scatter.30
  372.8 60.2 reduce-scatter.32
  436.7 66.8 reduce-scatter.20
  507.1 66.6 reduce-scatter.28
  577.3 66.6 reduce-scatter.12
  817.0 24.4 reduce-scatter.34
  844.3 24.8 reduce-scatter.26
  871.6 24.9 reduce-scatter.18
